TPU v7x, 32 devices: a whole 2x2x4 slice. The times are simulated.
32 devices in a mesh: dp: 4 (over x, core), expert: 8 (over z, y).
Axes of the slice: x: 2, y: 2, z: 4, core: 2. Of those that a mesh axis runs over, the one named last changes fastest.
Arguments:
- inputs: bfloat16 [512, 4096], P(('dp', 'expert')), may hold values from -6 to 6
- grad_out: bfloat16 [512, 4096], P(('dp', 'expert')), may hold values from -0.796875 to 0.796875
- labels: int32 [512, 1], P(('dp', 'expert')), may hold values from 0 to 7; in each aligned block of 16 rows (0 to 15, 16 to 31, ...) at most 3 rows name the same one
- w_gate: bfloat16 [4096, 57344], P('dp', 'expert'), may hold values from -0.09375 to 0.09375
- w_up: bfloat16 [4096, 57344], P('dp', 'expert'), may hold values from -0.09375 to 0.09375
- w_down: bfloat16 [57344, 4096], P('expert', 'dp'), may hold values from -0.0625 to 0.0625
Outputs:
- grad_in: bfloat16 [512, 4096], P(('dp', 'expert'))
- grad_gate: bfloat16 [4096, 57344], P('dp', 'expert')
- grad_up: bfloat16 [4096, 57344], P('dp', 'expert')
- grad_down: bfloat16 [57344, 4096], P('expert', 'dp')
Inputs may be any that keep to these rules, and one draw needn't show every extreme that they name: `labels`: among the 16 rows of one device no expert is named by more than 3 rows, a bound that some block reaches.
All inputs are finite; a program needn't handle non-finite values.
Results may differ from a plain program's by a relative error of at most 0.011.
Values may be sent and summed in bfloat16 or wider, within the bound.
No kernel may reach another device: no remote copies, remote signals or barrier semaphores. Data moves between devices by JAX's collectives and lax.ppermute only.
A program may use at most 192 MiB of HBM per device.

v0:
```python
import jax
import jax.numpy as jnp
from jax import lax
from jax.sharding import PartitionSpec as P

EXPERTS = 8


def nonlinear(gate, up, dhid):
    sig = jax.nn.sigmoid(gate)
    act = gate * sig
    hidden = (act * up).astype(jnp.bfloat16)
    d_up = (dhid * act).astype(jnp.bfloat16)
    d_gate = (dhid * up * sig * (1.0 + gate * (1.0 - sig))).astype(jnp.bfloat16)
    return (hidden, d_up, d_gate)


def contract_rows(left, right):
    return lax.dot_general(
        left, right, (((0,), (0,)), ((), ())), preferred_element_type=jnp.float32
    )


def on_device(inputs, grad_out, labels, w_gate, w_up, w_down):
    members = lax.axis_size("expert")
    replicas = lax.axis_size("dp")
    group = members // EXPERTS
    tok_count = inputs.shape[0]
    width = inputs.shape[1]
    capacity = 3 * tok_count // (2 * EXPERTS)
    label_col = labels[:, 0]
    onehot = (label_col[:, None] == jnp.arange(EXPERTS, dtype=jnp.int32)[None, :]).astype(jnp.int32)
    before = jnp.cumsum(onehot, axis=0) - onehot
    rank_in = jnp.sum(before * onehot, axis=1)
    slot_ids = label_col * capacity + rank_in

    def spread(values):
        buffer = jnp.zeros((EXPERTS * capacity, width), jnp.bfloat16).at[slot_ids].set(values)
        return jnp.repeat(buffer.reshape(EXPERTS, 1, capacity, width), group, axis=0)

    recv_in, recv_grad = (
        lax.all_to_all(
            lax.all_to_all(spread(inputs), "dp", split_axis=3, concat_axis=1, tiled=True),
            "expert",
            split_axis=0,
            concat_axis=0,
            tiled=True,
        ),
        lax.all_to_all(
            lax.all_to_all(spread(grad_out), "dp", split_axis=3, concat_axis=1, tiled=True),
            "expert",
            split_axis=0,
            concat_axis=0,
            tiled=True,
        ),
    )
    columns = width // replicas
    rows_in = recv_in.reshape(-1, columns)
    rows_grad = recv_grad.reshape(-1, columns)
    gate_part = jnp.dot(rows_in, w_gate, preferred_element_type=jnp.float32)
    up_part = jnp.dot(rows_in, w_up, preferred_element_type=jnp.float32)
    dhid_part = lax.dot_general(
        rows_grad, w_down, (((1,), (1,)), ((), ())), preferred_element_type=jnp.float32
    )
    gate, up, dhid = lax.psum((gate_part, up_part, dhid_part), "dp")
    hidden, d_up, d_gate = nonlinear(gate, up, dhid)
    d_rows = lax.dot_general(
        d_gate, w_gate, (((1,), (1,)), ((), ())), preferred_element_type=jnp.float32
    )
    d_rows = d_rows + lax.dot_general(
        d_up, w_up, (((1,), (1,)), ((), ())), preferred_element_type=jnp.float32
    )
    back_rows = lax.all_to_all(
        lax.all_to_all(
            d_rows.reshape(members, replicas, capacity, columns).astype(jnp.bfloat16),
            "dp",
            split_axis=1,
            concat_axis=3,
            tiled=True,
        ),
        "expert",
        split_axis=0,
        concat_axis=0,
        tiled=True,
    ).astype(jnp.float32)
    summed = jnp.sum(back_rows.reshape(EXPERTS, group, capacity, width), axis=1)
    grad_in = summed.reshape(EXPERTS * capacity, width)[slot_ids].astype(jnp.bfloat16)
    grad_gate = contract_rows(rows_in, d_gate).astype(jnp.bfloat16)
    grad_up = contract_rows(rows_in, d_up).astype(jnp.bfloat16)
    grad_down = contract_rows(hidden, rows_grad).astype(jnp.bfloat16)
    return (grad_in, grad_gate, grad_up, grad_down)


def solution(mesh):
    return jax.shard_map(
        on_device,
        mesh=mesh,
        in_specs=(
            P(("dp", "expert"), None),
            P(("dp", "expert"), None),
            P(("dp", "expert"), None),
            P("dp", "expert"),
            P("dp", "expert"),
            P("expert", "dp"),
        ),
        out_specs=(
            P(("dp", "expert"), None),
            P("dp", "expert"),
            P("dp", "expert"),
            P("expert", "dp"),
        ),
        check_vma=False,
    )
```

profile of v0, /device:TPU:0, one launch (start us, length us, event | category | flops | bytes accessed | tf_op | source)
XLA Modules:
  0.0 330.5 jit_solution(10850027350697886702)
XLA Ops:
  7.2 0.7 fusion.7
  7.9 0.8 select_reduce_fusion
  8.8 0.7 fusion.8
  9.4 1.2 scatter_custom_fusion.1
  10.8 4.6 %copy.38 = bf16[8,1,3,4096]{0,2,1,3:T(4,128)(2,1)} copy(bf16[8,1,3,4096]{3,2,0,1:T(4,128)(2,1)S(1)} %reshape_broadcast_in_dim_reshape.7) | data formatting | bytes 393216 | tf_op jit(solution)/shard_map/reshape;broadcast_in_dim;reshape | solution.py:39
  15.4 5.8 %reshape.60 = bf16[4,2,12288]{2,1,0:T(2,128)(2,1)} reshape(bf16[4096,1,3,8]{3,2,1,0:T(4,128)(2,1)} %bitcast.43) | data formatting | bytes 393216
  21.2 4.2 %all-to-all-start.2 = ((bf16[4,2,12288]{2,1,0:T(2,128)(2,1)}), bf16[4,2,12288]{2,1,0:T(2,128)(2,1)S(1)}, u32[]{:S(2)}, u32[]{:S(2)}) async-start(bf16[4,2,12288]{2,1,0:T(2,128)(2,1)} %reshape.60), calls=%async_computation.2 | async-start | bytes 393216 | tf_op jit(solution)/shard_map/all_to_all | solution.py:43
  25.4 1.2 scatter_custom_fusion
  26.8 4.6 %copy.34 = bf16[8,1,3,4096]{0,2,1,3:T(4,128)(2,1)} copy(bf16[8,1,3,4096]{3,2,0,1:T(4,128)(2,1)S(1)} %reshape_broadcast_in_dim_reshape.6) | data formatting | bytes 393216 | tf_op jit(solution)/shard_map/reshape;broadcast_in_dim;reshape | solution.py:39
  31.4 5.8 %reshape.62 = bf16[4,2,12288]{2,1,0:T(2,128)(2,1)} reshape(bf16[4096,1,3,8]{3,2,1,0:T(4,128)(2,1)} %bitcast.44) | data formatting | bytes 393216
  37.2 3.4 %all-to-all-start = ((bf16[4,2,12288]{2,1,0:T(2,128)(2,1)}), bf16[4,2,12288]{2,1,0:T(2,128)(2,1)S(1)}, u32[]{:S(2)}, u32[]{:S(2)}) async-start(bf16[4,2,12288]{2,1,0:T(2,128)(2,1)} %reshape.62), calls=%async_computation | async-start | bytes 393216 | tf_op jit(solution)/shard_map/all_to_all | solution.py:50
  40.6 4.8 %reshape.61 = bf16[4096,1,3,8]{3,2,1,0:T(4,128)(2,1)} reshape(bf16[4,2,12288]{2,1,0:T(2,128)(2,1)S(1)} %all-to-all-done.2) | data formatting | bytes 393216
  45.4 6.6 %copy.40 = bf16[8,4,3,1024]{3,1,2,0:T(4,128)(2,1)} copy(bf16[8,4,3,1024]{0,2,3,1:T(4,128)(2,1)} %bitcast.45) | data formatting | bytes 393216 | tf_op jit(solution)/shard_map/all_to_all | solution.py:43
  52.0 6.5 %all-to-all-start.3 = ((bf16[8,4,3,1024]{3,1,2,0:T(4,128)(2,1)}), bf16[8,4,3,1024]{3,1,2,0:T(4,128)(2,1)S(1)}, u32[]{:S(2)}, u32[]{:S(2)}) async-start(bf16[8,4,3,1024]{3,1,2,0:T(4,128)(2,1)} %copy.40), calls=%async_computation.3 | async-start | bytes 393216 | tf_op jit(solution)/shard_map/all_to_all | solution.py:42
  58.5 4.8 %reshape.63 = bf16[4096,1,3,8]{3,2,1,0:T(4,128)(2,1)} reshape(bf16[4,2,12288]{2,1,0:T(2,128)(2,1)S(1)} %all-to-all-done) | data formatting | bytes 393216
  63.2 6.7 %copy.36 = bf16[8,4,3,1024]{3,1,2,0:T(4,128)(2,1)} copy(bf16[8,4,3,1024]{0,2,3,1:T(4,128)(2,1)} %bitcast.46) | data formatting | bytes 393216 | tf_op jit(solution)/shard_map/all_to_all | solution.py:50
  69.9 6.0 %all-to-all-start.1 = ((bf16[8,4,3,1024]{3,1,2,0:T(4,128)(2,1)}), bf16[8,4,3,1024]{3,1,2,0:T(4,128)(2,1)S(1)}, u32[]{:S(2)}, u32[]{:S(2)}) async-start(bf16[8,4,3,1024]{3,1,2,0:T(4,128)(2,1)} %copy.36), calls=%async_computation.1 | async-start | bytes 393216 | tf_op jit(solution)/shard_map/all_to_all | solution.py:49
  76.4 9.2 %fusion.12 = f32[96,7168]{1,0:T(8,128)} fusion(bf16[96,1024]{1,0:T(8,128)(2,1)S(1)} %reshape.26, bf16[1024,7168]{1,0:T(8,128)(2,1)} %param.9), kind=kOutput, calls=%fused_computation.27 | convolution fusion | flops 1409286144 | bytes 17629184 | tf_op jit(solution)/shard_map/dot_general | solution.py:60
  85.6 9.2 %fusion.11 = f32[96,7168]{1,0:T(8,128)} fusion(bf16[96,1024]{1,0:T(8,128)(2,1)S(1)} %reshape.26, bf16[1024,7168]{1,0:T(8,128)(2,1)} %param.10), kind=kOutput, calls=%fused_computation.26 | convolution fusion | flops 1409286144 | bytes 17629184 | tf_op jit(solution)/shard_map/dot_general | solution.py:61
  95.0 11.3 %fusion.10 = f32[96,7168]{1,0:T(8,128)} fusion(bf16[96,1024]{1,0:T(8,128)(2,1)S(1)} %reshape.25, bf16[7168,1024]{1,0:T(8,128)(2,1)} %param.11), kind=kOutput, calls=%fused_computation.25 | convolution fusion | flops 1409286144 | bytes 17629184 | tf_op jit(solution)/shard_map/dot_general | solution.py:62
  106.4 153.3 %all-reduce.3.cloned.1.call-done = (f32[96,7168]{1,0:T(8,128)}, f32[96,7168]{1,0:T(8,128)}, f32[96,7168]{1,0:T(8,128)}) async-done(((f32[96,7168]{1,0:T(8,128)}, f32[96,7168]{1,0:T(8,128)}, f32[96,7168]{1,0:T(8,128)}), (f32[96,7168]{1,0:T(8,128)}, f32[96,7168]{1,0:T(8,128)}, f32[96,7168]{1,0:T(8,128)})) %all-reduce.3.cloned.1.call-update) | async-done | bytes 8257552 | tf_op jit(solution)/shard_map/psum | solution.py:65
  259.6 10.3 %convolution_convert_fusion = bf16[7168,1024]{1,0:T(8,128)(2,1)} fusion(bf16[96,1024]{1,0:T(8,128)(2,1)S(1)} %reshape.25, f32[96,7168]{1,0:T(8,128)} %get-tuple-element.6, f32[96,7168]{1,0:T(8,128)} %get-tuple-element.4), kind=kOutput, calls=%fused_computation.3 | convolution fusion | flops 1420754944 | bytes 20381696 | tf_op jit(solution)/shard_map/dot_general | solution.py:19
  270.0 4.0 %multiply_convert_fusion.1 = (bf16[96,7168]{1,0:T(8,128)(2,1)S(1)}, bf16[96,7168]{1,0:T(8,128)(2,1)S(1)}) fusion(f32[96,7168]{1,0:T(8,128)} %get-tuple-element.5, f32[96,7168]{1,0:T(8,128)S(1)} %copy-done, f32[96,7168]{1,0:T(8,128)} %get-tuple-element.6), kind=kLoop, calls=%fused_computation.7 | loop fusion | flops 8945664 | bytes 11010048 | tf_op jit(solution)/shard_map/convert_element_type | solution.py:13
  274.0 10.3 %fusion.13 = f32[96,1024]{1,0:T(8,128)S(1)} fusion(bf16[96,7168]{1,0:T(8,128)(2,1)S(1)} %get-tuple-element.8, bf16[1024,7168]{1,0:T(8,128)(2,1)} %param.9), kind=kOutput, calls=%fused_computation.28 | convolution fusion | flops 1409286144 | bytes 16449536 | tf_op jit(solution)/shard_map/dot_general | solution.py:67
  284.3 9.9 %fusion.1 = bf16[96,1024]{1,0:T(8,128)(2,1)S(1)} fusion(f32[96,1024]{1,0:T(8,128)S(1)} %fusion.13, bf16[96,7168]{1,0:T(8,128)(2,1)S(1)} %get-tuple-element.7, bf16[1024,7168]{1,0:T(8,128)(2,1)} %param.10), kind=kOutput, calls=%fused_computation.12 | convolution fusion | flops 1409482752 | bytes 16646144 | tf_op jit(solution)/shard_map/dot_general | solution.py:70
  294.3 0.8 copy.42
  295.1 3.6 %all-to-all-start.4 = ((bf16[8,4,3,1024]{3,0,2,1:T(8,128)(2,1)}), bf16[8,4,3,1024]{3,0,2,1:T(8,128)(2,1)S(1)}, u32[]{:S(2)}, u32[]{:S(2)}) async-start(bf16[8,4,3,1024]{3,0,2,1:T(8,128)(2,1)} %copy.42), calls=%async_computation.4 | async-start | bytes 393216 | tf_op jit(solution)/shard_map/all_to_all | solution.py:74
  298.8 7.6 %convolution_convert_fusion.1 = bf16[1024,7168]{1,0:T(8,128)(2,1)} fusion(bf16[96,1024]{1,0:T(8,128)(2,1)S(1)} %reshape.26, bf16[96,7168]{1,0:T(8,128)(2,1)S(1)} %get-tuple-element.7), kind=kOutput, calls=%fused_computation.4 | convolution fusion | flops 1416626176 | bytes 16252928 | tf_op jit(solution)/shard_map/dot_general | solution.py:19
  306.5 0.9 reshape.55
  307.4 5.5 %all-to-all-start.5 = ((bf16[8,1,3,4096]{3,2,1,0:T(4,128)(2,1)}), bf16[8,1,3,4096]{3,2,1,0:T(4,128)(2,1)S(1)}, u32[]{:S(2)}, u32[]{:S(2)}) async-start(bf16[8,1,3,4096]{3,2,1,0:T(4,128)(2,1)} %reshape.55), calls=%async_computation.5 | async-start | bytes 524288 | tf_op jit(solution)/shard_map/all_to_all | solution.py:73
  312.9 8.9 %convolution_convert_fusion.2 = bf16[1024,7168]{1,0:T(8,128)(2,1)} fusion(bf16[96,1024]{1,0:T(8,128)(2,1)S(1)} %reshape.26, bf16[96,7168]{1,0:T(8,128)(2,1)} %copy-done.1), kind=kOutput, calls=%fused_computation.5 | convolution fusion | flops 1416626176 | bytes 16252928 | tf_op jit(solution)/shard_map/dot_general | solution.py:19
  322.3 1.3 gather_fusion
  (23 shorter events, 2.0 us)
Async XLA Ops:
  21.2 16.0 %all-to-all-start.2 = ((bf16[4,2,12288]{2,1,0:T(2,128)(2,1)}), bf16[4,2,12288]{2,1,0:T(2,128)(2,1)S(1)}, u32[]{:S(2)}, u32[]{:S(2)}) async-start(bf16[4,2,12288]{2,1,0:T(2,128)(2,1)} %reshape.60), calls=%async_computation.2 | async-start | bytes 393216 | tf_op jit(solution)/shard_map/all_to_all | solution.py:43
  37.2 14.8 %all-to-all-start = ((bf16[4,2,12288]{2,1,0:T(2,128)(2,1)}), bf16[4,2,12288]{2,1,0:T(2,128)(2,1)S(1)}, u32[]{:S(2)}, u32[]{:S(2)}) async-start(bf16[4,2,12288]{2,1,0:T(2,128)(2,1)} %reshape.62), calls=%async_computation | async-start | bytes 393216 | tf_op jit(solution)/shard_map/all_to_all | solution.py:50
  52.0 17.9 %all-to-all-start.3 = ((bf16[8,4,3,1024]{3,1,2,0:T(4,128)(2,1)}), bf16[8,4,3,1024]{3,1,2,0:T(4,128)(2,1)S(1)}, u32[]{:S(2)}, u32[]{:S(2)}) async-start(bf16[8,4,3,1024]{3,1,2,0:T(4,128)(2,1)} %copy.40), calls=%async_computation.3 | async-start | bytes 393216 | tf_op jit(solution)/shard_map/all_to_all | solution.py:42
  69.9 24.8 %all-to-all-start.1 = ((bf16[8,4,3,1024]{3,1,2,0:T(4,128)(2,1)}), bf16[8,4,3,1024]{3,1,2,0:T(4,128)(2,1)S(1)}, u32[]{:S(2)}, u32[]{:S(2)}) async-start(bf16[8,4,3,1024]{3,1,2,0:T(4,128)(2,1)} %copy.36), calls=%async_computation.1 | async-start | bytes 393216 | tf_op jit(solution)/shard_map/all_to_all | solution.py:49
  75.9 183.8 %all-reduce.3.cloned.1.call-start = ((), (), s32[]{:S(2)}) async-start(), calls=%async_computation.6 | async-start | bytes 16515072 | tf_op jit(solution)/shard_map/psum | solution.py:65
  259.6 10.3 %copy-start = (f32[96,7168]{1,0:T(8,128)S(1)}, f32[96,7168]{1,0:T(8,128)}, u32[]{:S(2)}) copy-start(f32[96,7168]{1,0:T(8,128)} %get-tuple-element.4) | copy-start | bytes 8257540
  274.0 10.3 %copy-start.1 = (bf16[96,7168]{1,0:T(8,128)(2,1)}, bf16[96,7168]{1,0:T(8,128)(2,1)S(1)}, u32[]{:S(2)}) copy-start(bf16[96,7168]{1,0:T(8,128)(2,1)S(1)} %get-tuple-element.8) | copy-start | bytes 4128772
  295.1 11.2 %all-to-all-start.4 = ((bf16[8,4,3,1024]{3,0,2,1:T(8,128)(2,1)}), bf16[8,4,3,1024]{3,0,2,1:T(8,128)(2,1)S(1)}, u32[]{:S(2)}, u32[]{:S(2)}) async-start(bf16[8,4,3,1024]{3,0,2,1:T(8,128)(2,1)} %copy.42), calls=%async_computation.4 | async-start | bytes 393216 | tf_op jit(solution)/shard_map/all_to_all | solution.py:74
  307.4 14.8 %all-to-all-start.5 = ((bf16[8,1,3,4096]{3,2,1,0:T(4,128)(2,1)}), bf16[8,1,3,4096]{3,2,1,0:T(4,128)(2,1)S(1)}, u32[]{:S(2)}, u32[]{:S(2)}) async-start(bf16[8,1,3,4096]{3,2,1,0:T(4,128)(2,1)} %reshape.55), calls=%async_computation.5 | async-start | bytes 524288 | tf_op jit(solution)/shard_map/all_to_all | solution.py:73
Sparse Core Ops, SparseCore 0:
  106.5 153.1 all-reduce.2
where the time goes:
time: 332 us; the launch traced here: 330 us
  waiting for transfers between devices  154 us (46%)
  matrix products  76.6 us (23%)
  local copies, waits for them, and re-layouts  50.4 us (15%)
  starting transfers between devices  29.4 us (9%)
  between operations  14.2 us (4%)
  other arithmetic  6.24 us (2%)
    psum x1, waiting for transfers between devices, on_device(): gate, up, dhid = lax.psum((gate_part, up_part, dhid_part), 'dp')  153 us
    dot_general x3, matrix products, contract_rows(): lax.dot_general(left, right, (((0,), (0,)), ((), ())), preferred_element_...  26.9 us
    unnamed x8, local copies, waits for them, and re-layouts  21.2 us
    dot_general x1, matrix products, on_device(): lax.dot_general(rows_grad, w_down, (((1,), (1,)), ((), ())), preferred_el...  11.3 us
    dot_general x1, matrix products, on_device(): lax.dot_general(d_gate, w_gate, (((1,), (1,)), ((), ())), preferred_eleme...  10.3 us
    dot_general x1, matrix products, on_device(): lax.dot_general(d_up, w_up, (((1,), (1,)), ((), ())), preferred_element_t...  9.9 us
    another operation x4, local copies, waits for them, and re-layouts, spread(): jnp.repeat(buffer.reshape(EXPERTS, 1, capacity, width), group, axis=0)  9.43 us
    dot_general x1, matrix products, on_device(): gate_part = jnp.dot(rows_in, w_gate, preferred_element_type=jnp.float32)  9.16 us
  transfers between devices with their start and end apart: 7, of which 2 were waited for; matrix products, arithmetic and copies ran while one was open for 21% of the time, Pallas kernels for 0%

commit v1 on v0

--- a/solution.py
+++ b/solution.py
@@ -40,7 +40,12 @@
 
     recv_in, recv_grad = (
         lax.all_to_all(
-            lax.all_to_all(spread(inputs), "dp", split_axis=3, concat_axis=1, tiled=True),
+            jnp.concatenate(
+                lax.all_to_all(
+                    jnp.stack(jnp.split(spread(inputs), lax.axis_size("dp"), axis=3)), "dp", 0, 0
+                ),
+                axis=1,
+            ),
             "expert",
             split_axis=0,
             concat_axis=0,

time: 332 us -> 315 us (0.949)
  local copies, waits for them, and re-layouts: 50.4 us -> 30.3 us
    unnamed x8 -> x6, local copies, waits for them, and re-layouts: 21.2 us -> 10.6 us
    all_to_all x2 -> x1, local copies, waits for them, and re-layouts: 6.78 us -> 0.14 us  [on_device(): lax.all_to_all(jnp.concatenate(lax.all_to_all(jnp.stack(jnp.split(spread(...]
    another operation x4 -> x3, local copies, waits for them, and re-layouts: 9.43 us -> 4.84 us  [spread(): jnp.repeat(buffer.reshape(EXPERTS, 1, capacity, width), group, axis=0)]
    all_to_all x1, waiting for transfers between devices: 0.01 us -> 4.5 us  [on_device(): lax.all_to_all(spread(grad_out), 'dp', split_axis=3, concat_axis=1, tiled...]
  transfers between devices with their start and end apart: 7 -> 7, of which waited for: 2 -> 3; matrix products, arithmetic and copies ran while one was open for 21% -> 19% of each run, Pallas kernels for 0% -> 0%
where the time goes in v1:
time: 315 us; the launch traced here: 314 us
  waiting for transfers between devices  157 us (50%)
  matrix products  76.6 us (24%)
  local copies, waits for them, and re-layouts  30.3 us (10%)
  starting transfers between devices  29.3 us (9%)
  between operations  14.2 us (5%)
  other arithmetic  6.47 us (2%)
    psum x1, waiting for transfers between devices, on_device(): gate, up, dhid = lax.psum((gate_part, up_part, dhid_part), 'dp')  152 us
    dot_general x3, matrix products, contract_rows(): lax.dot_general(left, right, (((0,), (0,)), ((), ())), preferred_element_...  26.9 us
    dot_general x1, matrix products, on_device(): lax.dot_general(rows_grad, w_down, (((1,), (1,)), ((), ())), preferred_el...  11.3 us
    unnamed x6, local copies, waits for them, and re-layouts  10.6 us
    dot_general x1, matrix products, on_device(): lax.dot_general(d_gate, w_gate, (((1,), (1,)), ((), ())), preferred_eleme...  10.3 us
    dot_general x1, matrix products, on_device(): lax.dot_general(d_up, w_up, (((1,), (1,)), ((), ())), preferred_element_t...  9.9 us
    dot_general x1, matrix products, on_device(): gate_part = jnp.dot(rows_in, w_gate, preferred_element_type=jnp.float32)  9.16 us
    dot_general x1, matrix products, on_device(): up_part = jnp.dot(rows_in, w_up, preferred_element_type=jnp.float32)  9.15 us
  transfers between devices with their start and end apart: 7, of which 3 were waited for; matrix products, arithmetic and copies ran while one was open for 19% of the time, Pallas kernels for 0%

profile of v1, /device:TPU:0, one launch (start us, length us, event | category | flops | bytes accessed | tf_op | source)
XLA Modules:
  0.0 313.6 jit_solution(10159242219773479591)
XLA Ops:
  7.2 0.7 fusion.7
  7.9 0.8 select_reduce_fusion
  8.8 0.7 fusion.8
  9.4 1.2 scatter_custom_fusion.1
  11.1 0.8 copy.35
  11.9 4.2 %all-to-all-start.2 = ((bf16[4,8,1,3,1024]{4,1,3,2,0:T(8,128)(2,1)}), bf16[4,8,1,3,1024]{4,1,3,2,0:T(8,128)(2,1)S(1)}, u32[]{:S(2)}, u32[]{:S(2)}) async-start(bf16[4,8,1,3,1024]{4,1,3,2,0:T(8,128)(2,1)} %copy.35), calls=%async_computation.2 | async-start | bytes 393216 | tf_op jit(solution)/shard_map/all_to_all | solution.py:44
  16.1 1.2 scatter_custom_fusion
  17.4 4.6 %copy.31 = bf16[8,1,3,4096]{0,2,1,3:T(4,128)(2,1)} copy(bf16[8,1,3,4096]{3,2,0,1:T(4,128)(2,1)S(1)} %reshape_broadcast_in_dim_reshape.6) | data formatting | bytes 393216 | tf_op jit(solution)/shard_map/reshape;broadcast_in_dim;reshape | solution.py:39
  22.0 5.8 %reshape.68 = bf16[4,2,12288]{2,1,0:T(2,128)(2,1)} reshape(bf16[4096,1,3,8]{3,2,1,0:T(4,128)(2,1)} %bitcast.47) | data formatting | bytes 393216
  27.9 3.4 %all-to-all-start = ((bf16[4,2,12288]{2,1,0:T(2,128)(2,1)}), bf16[4,2,12288]{2,1,0:T(2,128)(2,1)S(1)}, u32[]{:S(2)}, u32[]{:S(2)}) async-start(bf16[4,2,12288]{2,1,0:T(2,128)(2,1)} %reshape.68), calls=%async_computation | async-start | bytes 393216 | tf_op jit(solution)/shard_map/all_to_all | solution.py:55
  31.3 0.8 copy.36
  32.1 4.5 %all-to-all-done = bf16[4,2,12288]{2,1,0:T(2,128)(2,1)S(1)} async-done(((bf16[4,2,12288]{2,1,0:T(2,128)(2,1)}), bf16[4,2,12288]{2,1,0:T(2,128)(2,1)S(1)}, u32[]{:S(2)}, u32[]{:S(2)}) %all-to-all-start) | async-done | bytes 196640 | tf_op jit(solution)/shard_map/all_to_all | solution.py:55
  36.6 6.4 %all-to-all-start.3 = ((bf16[8,4,3,1024]{3,1,2,0:T(4,128)(2,1)}), bf16[8,4,3,1024]{3,1,2,0:T(4,128)(2,1)S(1)}, u32[]{:S(2)}, u32[]{:S(2)}) async-start(bf16[8,4,3,1024]{3,1,2,0:T(4,128)(2,1)} %copy.36), calls=%async_computation.3 | async-start | bytes 393216 | tf_op jit(solution)/shard_map/all_to_all | solution.py:42
  43.0 4.8 %reshape.69 = bf16[4096,1,3,8]{3,2,1,0:T(4,128)(2,1)} reshape(bf16[4,2,12288]{2,1,0:T(2,128)(2,1)S(1)} %all-to-all-done) | data formatting | bytes 393216
  47.8 6.7 %copy.33 = bf16[8,4,3,1024]{3,1,2,0:T(4,128)(2,1)} copy(bf16[8,4,3,1024]{0,2,3,1:T(4,128)(2,1)} %bitcast.48) | data formatting | bytes 393216 | tf_op jit(solution)/shard_map/all_to_all | solution.py:55
  54.4 6.0 %all-to-all-start.1 = ((bf16[8,4,3,1024]{3,1,2,0:T(4,128)(2,1)}), bf16[8,4,3,1024]{3,1,2,0:T(4,128)(2,1)S(1)}, u32[]{:S(2)}, u32[]{:S(2)}) async-start(bf16[8,4,3,1024]{3,1,2,0:T(4,128)(2,1)} %copy.33), calls=%async_computation.1 | async-start | bytes 393216 | tf_op jit(solution)/shard_map/all_to_all | solution.py:54
  61.0 9.2 %fusion.12 = f32[96,7168]{1,0:T(8,128)} fusion(bf16[96,1024]{1,0:T(8,128)(2,1)S(1)} %reshape.34, bf16[1024,7168]{1,0:T(8,128)(2,1)} %param.9), kind=kOutput, calls=%fused_computation.32 | convolution fusion | flops 1409286144 | bytes 17629184 | tf_op jit(solution)/shard_map/dot_general | solution.py:65
  70.1 9.2 %fusion.11 = f32[96,7168]{1,0:T(8,128)} fusion(bf16[96,1024]{1,0:T(8,128)(2,1)S(1)} %reshape.34, bf16[1024,7168]{1,0:T(8,128)(2,1)} %param.10), kind=kOutput, calls=%fused_computation.31 | convolution fusion | flops 1409286144 | bytes 17629184 | tf_op jit(solution)/shard_map/dot_general | solution.py:66
  79.6 11.3 %fusion.10 = f32[96,7168]{1,0:T(8,128)} fusion(bf16[96,1024]{1,0:T(8,128)(2,1)S(1)} %reshape.31, bf16[7168,1024]{1,0:T(8,128)(2,1)} %param.11), kind=kOutput, calls=%fused_computation.30 | convolution fusion | flops 1409286144 | bytes 17629184 | tf_op jit(solution)/shard_map/dot_general | solution.py:67
  90.9 151.9 %all-reduce.3.cloned.1.call-done = (f32[96,7168]{1,0:T(8,128)}, f32[96,7168]{1,0:T(8,128)}, f32[96,7168]{1,0:T(8,128)}) async-done(((f32[96,7168]{1,0:T(8,128)}, f32[96,7168]{1,0:T(8,128)}, f32[96,7168]{1,0:T(8,128)}), (f32[96,7168]{1,0:T(8,128)}, f32[96,7168]{1,0:T(8,128)}, f32[96,7168]{1,0:T(8,128)})) %all-reduce.3.cloned.1.call-update) | async-done | bytes 8257552 | tf_op jit(solution)/shard_map/psum | solution.py:70
  242.8 10.3 %convolution_convert_fusion = bf16[7168,1024]{1,0:T(8,128)(2,1)} fusion(bf16[96,1024]{1,0:T(8,128)(2,1)S(1)} %reshape.31, f32[96,7168]{1,0:T(8,128)} %get-tuple-element.6, f32[96,7168]{1,0:T(8,128)} %get-tuple-element.4), kind=kOutput, calls=%fused_computation.3 | convolution fusion | flops 1420754944 | bytes 20381696 | tf_op jit(solution)/shard_map/dot_general | solution.py:19
  253.1 4.0 %multiply_convert_fusion.1 = (bf16[96,7168]{1,0:T(8,128)(2,1)S(1)}, bf16[96,7168]{1,0:T(8,128)(2,1)S(1)}) fusion(f32[96,7168]{1,0:T(8,128)} %get-tuple-element.5, f32[96,7168]{1,0:T(8,128)S(1)} %copy-done, f32[96,7168]{1,0:T(8,128)} %get-tuple-element.6), kind=kLoop, calls=%fused_computation.7 | loop fusion | flops 8945664 | bytes 11010048 | tf_op jit(solution)/shard_map/convert_element_type | solution.py:13
  257.1 10.3 %fusion.13 = f32[96,1024]{1,0:T(8,128)S(1)} fusion(bf16[96,7168]{1,0:T(8,128)(2,1)S(1)} %get-tuple-element.8, bf16[1024,7168]{1,0:T(8,128)(2,1)} %param.9), kind=kOutput, calls=%fused_computation.33 | convolution fusion | flops 1409286144 | bytes 16449536 | tf_op jit(solution)/shard_map/dot_general | solution.py:72
  267.4 9.9 %fusion.1 = bf16[96,1024]{1,0:T(8,128)(2,1)S(1)} fusion(f32[96,1024]{1,0:T(8,128)S(1)} %fusion.13, bf16[96,7168]{1,0:T(8,128)(2,1)S(1)} %get-tuple-element.7, bf16[1024,7168]{1,0:T(8,128)(2,1)} %param.10), kind=kOutput, calls=%fused_computation.12 | convolution fusion | flops 1409482752 | bytes 16646144 | tf_op jit(solution)/shard_map/dot_general | solution.py:75
  277.4 0.8 copy.38
  278.3 3.6 %all-to-all-start.4 = ((bf16[8,4,3,1024]{3,0,2,1:T(8,128)(2,1)}), bf16[8,4,3,1024]{3,0,2,1:T(8,128)(2,1)S(1)}, u32[]{:S(2)}, u32[]{:S(2)}) async-start(bf16[8,4,3,1024]{3,0,2,1:T(8,128)(2,1)} %copy.38), calls=%async_computation.4 | async-start | bytes 393216 | tf_op jit(solution)/shard_map/all_to_all | solution.py:79
  281.9 7.6 %convolution_convert_fusion.1 = bf16[1024,7168]{1,0:T(8,128)(2,1)} fusion(bf16[96,1024]{1,0:T(8,128)(2,1)S(1)} %reshape.34, bf16[96,7168]{1,0:T(8,128)(2,1)S(1)} %get-tuple-element.7), kind=kOutput, calls=%fused_computation.4 | convolution fusion | flops 1416626176 | bytes 16252928 | tf_op jit(solution)/shard_map/dot_general | solution.py:19
  289.6 0.9 reshape.63
  290.5 5.5 %all-to-all-start.5 = ((bf16[8,1,3,4096]{3,2,1,0:T(4,128)(2,1)}), bf16[8,1,3,4096]{3,2,1,0:T(4,128)(2,1)S(1)}, u32[]{:S(2)}, u32[]{:S(2)}) async-start(bf16[8,1,3,4096]{3,2,1,0:T(4,128)(2,1)} %reshape.63), calls=%async_computation.5 | async-start | bytes 524288 | tf_op jit(solution)/shard_map/all_to_all | solution.py:78
  296.0 8.9 %convolution_convert_fusion.2 = bf16[1024,7168]{1,0:T(8,128)(2,1)} fusion(bf16[96,1024]{1,0:T(8,128)(2,1)S(1)} %reshape.34, bf16[96,7168]{1,0:T(8,128)(2,1)} %copy-done.1), kind=kOutput, calls=%fused_computation.5 | convolution fusion | flops 1416626176 | bytes 16252928 | tf_op jit(solution)/shard_map/dot_general | solution.py:19
  305.0 0.3 all-to-all-done.5
  305.5 1.3 gather_fusion
  (23 shorter events, 1.9 us)
Async XLA Ops:
  11.9 16.0 %all-to-all-start.2 = ((bf16[4,8,1,3,1024]{4,1,3,2,0:T(8,128)(2,1)}), bf16[4,8,1,3,1024]{4,1,3,2,0:T(8,128)(2,1)S(1)}, u32[]{:S(2)}, u32[]{:S(2)}) async-start(bf16[4,8,1,3,1024]{4,1,3,2,0:T(8,128)(2,1)} %copy.35), calls=%async_computation.2 | async-start | bytes 393216 | tf_op jit(solution)/shard_map/all_to_all | solution.py:44
  27.9 8.7 %all-to-all-start = ((bf16[4,2,12288]{2,1,0:T(2,128)(2,1)}), bf16[4,2,12288]{2,1,0:T(2,128)(2,1)S(1)}, u32[]{:S(2)}, u32[]{:S(2)}) async-start(bf16[4,2,12288]{2,1,0:T(2,128)(2,1)} %reshape.68), calls=%async_computation | async-start | bytes 393216 | tf_op jit(solution)/shard_map/all_to_all | solution.py:55
  36.6 17.8 %all-to-all-start.3 = ((bf16[8,4,3,1024]{3,1,2,0:T(4,128)(2,1)}), bf16[8,4,3,1024]{3,1,2,0:T(4,128)(2,1)S(1)}, u32[]{:S(2)}, u32[]{:S(2)}) async-start(bf16[8,4,3,1024]{3,1,2,0:T(4,128)(2,1)} %copy.36), calls=%async_computation.3 | async-start | bytes 393216 | tf_op jit(solution)/shard_map/all_to_all | solution.py:42
  54.4 24.8 %all-to-all-start.1 = ((bf16[8,4,3,1024]{3,1,2,0:T(4,128)(2,1)}), bf16[8,4,3,1024]{3,1,2,0:T(4,128)(2,1)S(1)}, u32[]{:S(2)}, u32[]{:S(2)}) async-start(bf16[8,4,3,1024]{3,1,2,0:T(4,128)(2,1)} %copy.33), calls=%async_computation.1 | async-start | bytes 393216 | tf_op jit(solution)/shard_map/all_to_all | solution.py:54
  60.4 182.4 %all-reduce.3.cloned.1.call-start = ((), (), s32[]{:S(2)}) async-start(), calls=%async_computation.6 | async-start | bytes 16515072 | tf_op jit(solution)/shard_map/psum | solution.py:70
  242.8 10.3 %copy-start = (f32[96,7168]{1,0:T(8,128)S(1)}, f32[96,7168]{1,0:T(8,128)}, u32[]{:S(2)}) copy-start(f32[96,7168]{1,0:T(8,128)} %get-tuple-element.4) | copy-start | bytes 8257540
  257.1 10.3 %copy-start.1 = (bf16[96,7168]{1,0:T(8,128)(2,1)}, bf16[96,7168]{1,0:T(8,128)(2,1)S(1)}, u32[]{:S(2)}) copy-start(bf16[96,7168]{1,0:T(8,128)(2,1)S(1)} %get-tuple-element.8) | copy-start | bytes 4128772
  278.3 11.2 %all-to-all-start.4 = ((bf16[8,4,3,1024]{3,0,2,1:T(8,128)(2,1)}), bf16[8,4,3,1024]{3,0,2,1:T(8,128)(2,1)S(1)}, u32[]{:S(2)}, u32[]{:S(2)}) async-start(bf16[8,4,3,1024]{3,0,2,1:T(8,128)(2,1)} %copy.38), calls=%async_computation.4 | async-start | bytes 393216 | tf_op jit(solution)/shard_map/all_to_all | solution.py:79
  290.5 14.8 %all-to-all-start.5 = ((bf16[8,1,3,4096]{3,2,1,0:T(4,128)(2,1)}), bf16[8,1,3,4096]{3,2,1,0:T(4,128)(2,1)S(1)}, u32[]{:S(2)}, u32[]{:S(2)}) async-start(bf16[8,1,3,4096]{3,2,1,0:T(4,128)(2,1)} %reshape.63), calls=%async_computation.5 | async-start | bytes 524288 | tf_op jit(solution)/shard_map/all_to_all | solution.py:78
Sparse Core Ops, SparseCore 0:
  91.0 151.7 all-reduce.2
